TPU v7x, 512 devices: a whole 4x4x16 slice. The times are simulated.
512 devices in a mesh: blk: 64 (over y_lo, z, core), exp: 8 (over y_hi, x).
Axes of the slice: x: 4, y: 4 (y_hi: 2, y_lo: 2; y = y_hi * 2 + y_lo), z: 16, core: 2. Of those that a mesh axis runs over, the one named last changes fastest.
Arguments:
- hidden_in: bfloat16 [32, 4, 2048], P('exp'), may hold values from -3 to 3
- q_lat: bfloat16 [32, 4, 16, 512], P('exp'), may hold values from -28 to 28
- q_rope: bfloat16 [32, 4, 16, 64], P('exp'), may hold values from -4 to 4
- new_lat: bfloat16 [32, 4, 512], P('exp'), may hold values from -4 to 4
- new_rope: bfloat16 [32, 4, 64], P('exp'), may hold values from -4 to 4
- cache_lat: bfloat16 [32, 16384, 512], P('exp', 'blk'), may hold values from -4 to 4
- cache_rope: bfloat16 [32, 16384, 64], P('exp', 'blk'), may hold values from -4 to 4
- lengths: int32 [32], P('exp'), may hold values from 2 to 16384, as said below
- w_uv: bfloat16 [512, 2048], P(None, 'blk'), may hold values from -3 to 3
- w_out: bfloat16 [2048, 2048], P('blk'), may hold values from -0.125 to 0.125
- norm_gain: float32 [2048], replicated, may hold values from 0.1 to 1.9
- w_router: bfloat16 [2048, 64], replicated, may hold values from -0.125 to 0.125
- routes: int32 [32, 4, 6], P('exp'), may hold values from 0 to 63, all different within a row; in each aligned block of 16 rows (0 to 15, 16 to 31, ..., all dimensions but the last counted through in order) at most 3 rows name the same one
- w_gate: bfloat16 [64, 2048, 1408], P('blk', None, 'exp'), may hold values from -0.125 to 0.125
- w_up: bfloat16 [64, 2048, 1408], P('blk', None, 'exp'), may hold values from -0.125 to 0.125
- w_down: bfloat16 [64, 1408, 2048], P('blk', 'exp'), may hold values from -0.15625 to 0.15625
Outputs:
- hidden_out: bfloat16 [32, 4, 2048], P('exp')
Inputs may be any that keep to these rules, and one draw needn't show every extreme that they name: `lengths`: in each aligned group of 4 requests exactly 1 have length 16384; the others have 2 to 512. `routes`: each row names 6 different experts; in the 16 rows of one index of exp no expert is named more than 3 times.
All inputs are finite; a program needn't handle non-finite values.
Results may differ from a plain program's by a relative error of at most 0.0062.
Values may be sent and summed in bfloat16 or wider, within the bound.
No kernel may reach another device: no remote copies, remote signals or barrier semaphores. Data moves between devices by JAX's collectives and lax.ppermute only.
A program may use at most 128 MiB of HBM per device.

v0:
```python
import jax
import jax.numpy as jnp
from jax import lax
from jax.sharding import PartitionSpec as P

V = 128
QK = 192
CAP = 3
NEG_FILL = -1e30
ROUTE_SCALE = 2.446
NORM_EPS = 1e-06


def xor_pairs(count, mask):
    return [(i, i ^ mask) for i in range(count)]


def exchange(x, axis, mask):
    count = lax.axis_size(axis)
    return jax.tree.map(lambda part: lax.ppermute(part, axis, xor_pairs(count, mask)), x)


def exchange_state(state, axis, mask):
    peak_val, weight_sum, summed = state
    packed = jnp.concatenate([summed, peak_val[..., None], weight_sum[..., None]], axis=-1)
    got = exchange(packed, axis, mask)
    width = summed.shape[-1]
    return (got[..., width], got[..., width + 1], got[..., :width])


def butterfly_sum(x, axis, bits):
    for bit in bits:
        x = x + exchange(x, axis, 1 << bit)
    return x


def butterfly_gather(x, axis, bits):
    me = lax.axis_index(axis)
    x = x[None]
    for bit in bits:
        other = exchange(x, axis, 1 << bit)
        high = me >> bit & 1 == 1
        low_part = jnp.where(high, other, x)
        high_part = jnp.where(high, x, other)
        x = jnp.concatenate([low_part, high_part], axis=0)
    return x


def butterfly_scatter_sum(x, axis, bits):
    me = lax.axis_index(axis)
    for bit in bits:
        side = me >> bit & 1
        keep = lax.dynamic_index_in_dim(x, side, 0, keepdims=False)
        send = lax.dynamic_index_in_dim(x, 1 - side, 0, keepdims=False)
        x = keep + exchange(send, axis, 1 << bit)
    return x


def block_partial(query, query_rope, keys_lat, keys_rope, valid):
    scale = QK ** (-0.5)
    scores = (
        jnp.einsum("rmc,rkc->rmk", query, keys_lat, preferred_element_type=jnp.float32)
        + jnp.einsum("rmc,rkc->rmk", query_rope, keys_rope, preferred_element_type=jnp.float32)
    ) * scale
    masked = jnp.where(valid, scores, NEG_FILL)
    peak_val = jnp.max(masked, axis=2)
    weights = jnp.where(valid, jnp.exp(masked - peak_val[:, :, None]), 0.0)
    weight_sum = jnp.sum(weights, axis=2)
    summed = jnp.einsum(
        "rmk,rkc->rmc", weights.astype(jnp.bfloat16), keys_lat, preferred_element_type=jnp.float32
    )
    return (peak_val, weight_sum, summed)


def merge_pair(left_part, right_part):
    peak_left, total_left, sum_left = left_part
    peak_right, total_right, sum_right = right_part
    peak_val = jnp.maximum(peak_left, peak_right)
    factor_left = jnp.exp(peak_left - peak_val)
    factor_right = jnp.exp(peak_right - peak_val)
    weight_sum = factor_left * total_left + factor_right * total_right
    summed = factor_left[..., None] * sum_left + factor_right[..., None] * sum_right
    return (peak_val, weight_sum, summed)


def local(
    hidden_in,
    q_lat,
    q_rope,
    new_lat,
    new_rope,
    cache_lat,
    cache_rope,
    lengths,
    w_uv,
    w_out,
    norm_gain,
    w_router,
    routes,
    w_gate,
    w_up,
    w_down,
):
    requests, new_steps, head_count, latent_dim = q_lat.shape
    me = lax.axis_index("blk")
    blk_bits = lax.axis_size("blk").bit_length() - 1
    exp_bits = lax.axis_size("exp").bit_length() - 1
    query_rows = new_steps * head_count
    query = q_lat.reshape(requests, query_rows, latent_dim)
    query_rope = q_rope.reshape(requests, query_rows, q_rope.shape[3])
    cache_span = cache_lat.shape[1]
    position = me * cache_span + lax.iota(jnp.int32, cache_span)
    cache_valid = jnp.broadcast_to(
        position[None, None, :] < lengths[:, None, None], (requests, query_rows, cache_span)
    )
    peak_val, weight_sum, summed = block_partial(
        query, query_rope, cache_lat, cache_rope, cache_valid
    )
    head_bits = head_count.bit_length() - 1
    split = (2,) * head_bits
    state = (
        peak_val.reshape(requests, new_steps, head_count)
        .transpose(2, 0, 1)
        .reshape(split + (requests, new_steps)),
        weight_sum.reshape(requests, new_steps, head_count)
        .transpose(2, 0, 1)
        .reshape(split + (requests, new_steps)),
        summed.reshape(requests, new_steps, head_count, latent_dim)
        .transpose(2, 0, 1, 3)
        .reshape(split + (requests, new_steps, latent_dim)),
    )
    low_bits = blk_bits - head_bits
    order = [head_bits - 1] + list(range(head_bits - 1))
    remaining = list(range(head_bits - 1, -1, -1))
    for head_bit in order:
        axis_pos = remaining.index(head_bit)
        remaining.pop(axis_pos)
        bit = head_bit + low_bits
        side = me >> bit & 1
        keep = jax.tree.map(
            lambda part: lax.dynamic_index_in_dim(part, side, axis_pos, keepdims=False), state
        )
        send = jax.tree.map(
            lambda part: lax.dynamic_index_in_dim(part, 1 - side, axis_pos, keepdims=False), state
        )
        state = merge_pair(keep, exchange_state(send, "blk", 1 << bit))
    for bit in range(low_bits - 1, -1, -1):
        state = merge_pair(state, exchange_state(state, "blk", 1 << bit))
    head_pick = me >> low_bits
    own_query = lax.dynamic_index_in_dim(q_lat, head_pick, axis=2, keepdims=False)
    own_rope = lax.dynamic_index_in_dim(q_rope, head_pick, axis=2, keepdims=False)
    fresh_valid = lax.iota(jnp.int32, new_steps)[None, :] <= lax.iota(jnp.int32, new_steps)[:, None]
    fresh_valid = jnp.broadcast_to(fresh_valid[None, :, :], (requests, new_steps, new_steps))
    fresh_part = block_partial(own_query, own_rope, new_lat, new_rope, fresh_valid)
    peak_val, weight_sum, summed = merge_pair(state, fresh_part)
    lat_out = (summed / weight_sum[:, :, None]).astype(jnp.bfloat16)
    token_rows = requests * new_steps
    lat_head = lat_out.reshape(token_rows, latent_dim)
    heads_out = jnp.dot(lat_head, w_uv, preferred_element_type=jnp.float32).astype(jnp.bfloat16)
    proj_part = jnp.dot(heads_out, w_out, preferred_element_type=jnp.float32)
    projected = butterfly_sum(proj_part, "blk", range(blk_bits))
    width = hidden_in.shape[2]
    mixed = hidden_in.reshape(token_rows, width).astype(jnp.float32) + projected
    meansq = jnp.mean(mixed * mixed, axis=1, keepdims=True)
    normed = (mixed * lax.rsqrt(meansq + NORM_EPS) * norm_gain[None, :]).astype(jnp.bfloat16)
    affinity = jax.nn.sigmoid(jnp.dot(normed, w_router, preferred_element_type=jnp.float32))
    expert_total = w_router.shape[1]
    top_count = routes.shape[2]
    flat_routes = routes.reshape(token_rows, top_count)
    route_hits = flat_routes[:, :, None] == lax.iota(jnp.int32, expert_total)[None, None, :]
    chosen = jnp.sum(jnp.where(route_hits, affinity[:, None, :], 0.0), axis=2)
    route_weight = ROUTE_SCALE * chosen / jnp.sum(chosen, axis=1, keepdims=True)
    local_count = w_gate.shape[0]
    local_ids = me * local_count + lax.iota(jnp.int32, local_count)
    pair_routes = flat_routes.reshape(token_rows * top_count)
    local_hits = (pair_routes[:, None] == local_ids[None, :]).astype(jnp.int32)
    ranks = jnp.cumsum(local_hits, axis=0) - 1
    slot_ids = lax.iota(jnp.int32, CAP)
    slot_match = local_hits.T[:, None, :] * (ranks.T[:, None, :] == slot_ids[None, :, None]).astype(
        jnp.int32
    )
    select = slot_match.reshape(local_count, CAP, token_rows, top_count).astype(jnp.float32)
    dispatch_map = jnp.sum(select, axis=3)
    combine_map = jnp.sum(select * route_weight[None, None, :, :], axis=3)
    dispatched = jnp.einsum(
        "esr,rd->esd", dispatch_map.astype(jnp.bfloat16), normed, preferred_element_type=jnp.float32
    ).astype(jnp.bfloat16)
    gate_w = lax.all_gather(w_gate, "exp", axis=2, tiled=True)
    up_w = lax.all_gather(w_up, "exp", axis=2, tiled=True)
    down_w = lax.all_gather(w_down, "exp", axis=1, tiled=True)
    gate = jnp.einsum("erd,edf->erf", dispatched, gate_w, preferred_element_type=jnp.float32)
    upper = jnp.einsum("erd,edf->erf", dispatched, up_w, preferred_element_type=jnp.float32)
    hidden_all = (jax.nn.silu(gate) * upper).astype(jnp.bfloat16)
    expert_out = jnp.einsum("erf,efd->erd", hidden_all, down_w, preferred_element_type=jnp.float32)
    moe_part = jnp.einsum("esr,esd->rd", combine_map, expert_out, precision=lax.Precision.HIGHEST)
    moe_all = butterfly_sum(moe_part, "blk", range(blk_bits))
    result = (mixed + moe_all).astype(jnp.bfloat16)
    return result.reshape(requests, new_steps, width)


def solution(mesh):
    in_specs = (
        P("exp", None, None),
        P("exp", None, None, None),
        P("exp", None, None, None),
        P("exp", None, None),
        P("exp", None, None),
        P("exp", "blk", None),
        P("exp", "blk", None),
        P("exp"),
        P(None, "blk"),
        P("blk", None),
        P(),
        P(),
        P("exp", None, None),
        P("blk", None, "exp"),
        P("blk", None, "exp"),
        P("blk", "exp", None),
    )
    out_specs = P("exp", None, None)
    return jax.shard_map(local, mesh=mesh, in_specs=in_specs, out_specs=out_specs, check_vma=False)
```

profile of v0, /device:TPU:8, one launch (start us, length us, event | category | flops | bytes accessed | tf_op | source)
XLA Modules:
  0.0 402.4 jit_solution(3735238704035035130)
XLA Ops:
  14.3 7.7 %collective-permute-start = (f32[2,2,2,4,4,514]{5,4,3,2,1,0:T(4,128)S(1)}, f32[2,2,2,4,4,514]{5,4,3,2,1,0:T(4,128)S(1)}, u32[]{:S(2)}, u32[]{:S(2)}) collective-permute-start(f32[2,2,2,4,4,514]{5,4,3,2,1,0:T(4,128)S(1)} %pad_maximum_fusion), channel_id=1, source_target_pairs={{0,256},{8,264},{16,272},{24,280},{32,288},{40,296},{48,304},{56,3... | collective-permute-start | bytes 789512 | tf_op jit(solution)/shard_map/ppermute | solution.py:20
  22.9 4.1 %collective-permute-done = f32[2,2,2,4,4,514]{5,4,3,2,1,0:T(4,128)S(1)} collective-permute-done((f32[2,2,2,4,4,514]{5,4,3,2,1,0:T(4,128)S(1)}, f32[2,2,2,4,4,514]{5,4,3,2,1,0:T(4,128)S(1)}, u32[]{:S(2)}, u32[]{:S(2)}) %collective-permute-start) | collective-permute-done | bytes 263200 | tf_op jit(solution)/shard_map/ppermute | solution.py:20
  32.2 6.7 %collective-permute-done.1 = f32[2,2,4,4,514]{4,3,2,1,0:T(4,128)S(1)} collective-permute-done((f32[2,2,4,4,514]{4,3,2,1,0:T(4,128)S(1)}, f32[2,2,4,4,514]{4,3,2,1,0:T(4,128)S(1)}, u32[]{:S(2)}, u32[]{:S(2)}) %collective-permute-start.1) | collective-permute-done | bytes 131616 | tf_op jit(solution)/shard_map/ppermute | solution.py:20
  39.8 9.1 %collective-permute-start.2 = (f32[2,4,4,514]{3,2,1,0:T(4,128)S(1)}, f32[2,4,4,514]{3,2,1,0:T(4,128)S(1)}, u32[]{:S(2)}, u32[]{:S(2)}) collective-permute-start(f32[2,4,4,514]{3,2,1,0:T(4,128)S(1)} %pad_maximum_fusion.2), channel_id=1, source_target_pairs={{0,64},{8,72},{16,80},{24,88},{32,96},{40,104},{48,112},{56,120},{... | collective-permute-start | bytes 197384 | tf_op jit(solution)/shard_map/ppermute | solution.py:20
  49.7 5.0 %collective-permute-done.2 = f32[2,4,4,514]{3,2,1,0:T(4,128)S(1)} collective-permute-done((f32[2,4,4,514]{3,2,1,0:T(4,128)S(1)}, f32[2,4,4,514]{3,2,1,0:T(4,128)S(1)}, u32[]{:S(2)}, u32[]{:S(2)}) %collective-permute-start.2) | collective-permute-done | bytes 65824 | tf_op jit(solution)/shard_map/ppermute | solution.py:20
  55.5 13.7 %collective-permute-start.3 = (f32[4,4,514]{2,1,0:T(4,128)S(1)}, f32[4,4,514]{2,1,0:T(4,128)S(1)}, u32[]{:S(2)}, u32[]{:S(2)}) collective-permute-start(f32[4,4,514]{2,1,0:T(4,128)S(1)} %pad_maximum_fusion.3), channel_id=1, source_target_pairs={{0,128},{8,136},{16,144},{24,152},{32,160},{40,168},{48,176},{56,1... | collective-permute-start | bytes 98696 | tf_op jit(solution)/shard_map/ppermute | solution.py:20
  73.6 3.8 collective-permute-done.4
  86.7 5.5 %collective-permute-done.7 = f32[16,2048]{1,0:T(8,128)S(1)} collective-permute-done((f32[16,2048]{1,0:T(8,128)S(1)}, f32[16,2048]{1,0:T(8,128)S(1)}, u32[]{:S(2)}, u32[]{:S(2)}) %collective-permute-start.7) | collective-permute-done | bytes 131104 | tf_op jit(solution)/shard_map/ppermute | solution.py:20
  94.2 8.5 %collective-permute-done.8 = f32[16,2048]{1,0:T(8,128)S(1)} collective-permute-done((f32[16,2048]{1,0:T(8,128)S(1)}, f32[16,2048]{1,0:T(8,128)S(1)}, u32[]{:S(2)}, u32[]{:S(2)}) %collective-permute-start.8) | collective-permute-done | bytes 131104 | tf_op jit(solution)/shard_map/ppermute | solution.py:20
  102.7 6.4 %collective-permute-start.9 = (f32[16,2048]{1,0:T(8,128)S(1)}, f32[16,2048]{1,0:T(8,128)S(1)}, u32[]{:S(2)}, u32[]{:S(2)}) collective-permute-start(f32[16,2048]{1,0:T(8,128)S(1)} %add.218), channel_id=1, source_target_pairs={{0,64},{8,72},{16,80},{24,88},{32,96},{40,104},{48,112},{56,120},{... | collective-permute-start | bytes 393224 | tf_op jit(solution)/shard_map/ppermute | solution.py:20
  109.1 12.2 %collective-permute-done.9 = f32[16,2048]{1,0:T(8,128)S(1)} collective-permute-done((f32[16,2048]{1,0:T(8,128)S(1)}, f32[16,2048]{1,0:T(8,128)S(1)}, u32[]{:S(2)}, u32[]{:S(2)}) %collective-permute-start.9) | collective-permute-done | bytes 131104 | tf_op jit(solution)/shard_map/ppermute | solution.py:20
  121.3 10.5 %collective-permute-start.10 = (f32[16,2048]{1,0:T(8,128)S(1)}, f32[16,2048]{1,0:T(8,128)S(1)}, u32[]{:S(2)}, u32[]{:S(2)}) collective-permute-start(f32[16,2048]{1,0:T(8,128)S(1)} %add.219), channel_id=1, source_target_pairs={{0,128},{8,136},{16,144},{24,152},{32,160},{40,168},{48,176},{56,1... | collective-permute-start | bytes 393224 | tf_op jit(solution)/shard_map/ppermute | solution.py:20
  131.9 12.3 %collective-permute-done.10 = f32[16,2048]{1,0:T(8,128)S(1)} collective-permute-done((f32[16,2048]{1,0:T(8,128)S(1)}, f32[16,2048]{1,0:T(8,128)S(1)}, u32[]{:S(2)}, u32[]{:S(2)}) %collective-permute-start.10) | collective-permute-done | bytes 131104 | tf_op jit(solution)/shard_map/ppermute | solution.py:20
  152.0 4.2 %fusion.4 = f32[3,1408]{1,0:T(4,128)S(1)} fusion(bf16[3,2048]{1,0:T(4,128)(2,1)S(1)} %convolution_convert_fusion, bf16[1,2048,1408]{1,2,0:T(8,128)(2,1)} %all-gather.4.cloned.1.call-done), kind=kOutput, calls=%fused_computation.4 | convolution fusion | flops 17301504 | bytes 5796352 | tf_op jit(solution)/shard_map/erd,edf->erf/dot_general | solution.py:191
  156.2 61.2 %all-gather.6.cloned.1.call-done = bf16[1,2048,1408]{1,2,0:T(8,128)(2,1)} async-done(((bf16[1,2048,176]{1,2,0:T(8,128)(2,1)}), bf16[1,2048,1408]{1,2,0:T(8,128)(2,1)}) %all-gather.6.cloned.1.call-update) | async-done | bytes 5767184 | tf_op jit(solution)/shard_map/all_gather | solution.py:189
  217.4 100.9 %all-gather.8.cloned.1.call-done = bf16[1,1408,2048]{2,1,0:T(8,128)(2,1)} async-done(((bf16[1,176,2048]{2,1,0:T(8,128)(2,1)}), bf16[1,1408,2048]{2,1,0:T(8,128)(2,1)}) %all-gather.8.cloned.1.call-update) | async-done | bytes 5767184 | tf_op jit(solution)/shard_map/all_gather | solution.py:190
  318.4 7.0 %fusion = f32[3,2048]{1,0:T(4,128)S(1)} fusion(bf16[1,1408,2048]{2,1,0:T(8,128)(2,1)} %all-gather.8.cloned.1.call-done, bf16[3,2048]{1,0:T(4,128)(2,1)S(1)} %convolution_convert_fusion, bf16[1,2048,1408]{1,2,0:T(8,128)(2,1)} %all-gather.6.cloned.1.call-done, f32[3,1408]{1,0:T(4,128)S(1)} %fusion.4), kind=kOutput, calls=%fused_computation | convolution fusion | flops 34628352 | bytes 11588096 | tf_op jit(solution)/shard_map/erf,efd->erd/dot_general | solution.py:194
  332.5 4.0 collective-permute-done.13
  336.5 4.5 %collective-permute-start.14 = (f32[16,2048]{1,0:T(8,128)S(1)}, f32[16,2048]{1,0:T(8,128)S(1)}, u32[]{:S(2)}, u32[]{:S(2)}) collective-permute-start(f32[16,2048]{1,0:T(8,128)S(1)} %add.227), channel_id=1, source_target_pairs={{0,32},{8,40},{16,48},{24,56},{32,0},{40,8},{48,16},{56,24},{64,96... | collective-permute-start | bytes 393224 | tf_op jit(solution)/shard_map/ppermute | solution.py:20
  340.9 5.8 %collective-permute-done.14 = f32[16,2048]{1,0:T(8,128)S(1)} collective-permute-done((f32[16,2048]{1,0:T(8,128)S(1)}, f32[16,2048]{1,0:T(8,128)S(1)}, u32[]{:S(2)}, u32[]{:S(2)}) %collective-permute-start.14) | collective-permute-done | bytes 131104 | tf_op jit(solution)/shard_map/ppermute | solution.py:20
  346.8 7.6 %collective-permute-start.15 = (f32[16,2048]{1,0:T(8,128)S(1)}, f32[16,2048]{1,0:T(8,128)S(1)}, u32[]{:S(2)}, u32[]{:S(2)}) collective-permute-start(f32[16,2048]{1,0:T(8,128)S(1)} %add.228), channel_id=1, source_target_pairs={{0,64},{8,72},{16,80},{24,88},{32,96},{40,104},{48,112},{56,120},{... | collective-permute-start | bytes 393224 | tf_op jit(solution)/shard_map/ppermute | solution.py:20
  354.4 9.9 %collective-permute-done.15 = f32[16,2048]{1,0:T(8,128)S(1)} collective-permute-done((f32[16,2048]{1,0:T(8,128)S(1)}, f32[16,2048]{1,0:T(8,128)S(1)}, u32[]{:S(2)}, u32[]{:S(2)}) %collective-permute-start.15) | collective-permute-done | bytes 131104 | tf_op jit(solution)/shard_map/ppermute | solution.py:20
  364.4 12.0 %collective-permute-start.16 = (f32[16,2048]{1,0:T(8,128)S(1)}, f32[16,2048]{1,0:T(8,128)S(1)}, u32[]{:S(2)}, u32[]{:S(2)}) collective-permute-start(f32[16,2048]{1,0:T(8,128)S(1)} %add.229), channel_id=1, source_target_pairs={{0,128},{8,136},{16,144},{24,152},{32,160},{40,168},{48,176},{56,1... | collective-permute-start | bytes 393224 | tf_op jit(solution)/shard_map/ppermute | solution.py:20
  376.4 12.0 %collective-permute-done.16 = f32[16,2048]{1,0:T(8,128)S(1)} collective-permute-done((f32[16,2048]{1,0:T(8,128)S(1)}, f32[16,2048]{1,0:T(8,128)S(1)}, u32[]{:S(2)}, u32[]{:S(2)}) %collective-permute-start.16) | collective-permute-done | bytes 131104 | tf_op jit(solution)/shard_map/ppermute | solution.py:20
  (142 shorter events, 54.1 us)
Async XLA Ops:
  6.5 145.5 %all-gather.4.cloned.1.call-start = ((), (), s32[]{:S(2)}) async-start(), calls=%async_computation | async-start | bytes 6488064 | tf_op jit(solution)/shard_map/all_gather | solution.py:188
  7.3 210.1 %all-gather.6.cloned.1.call-start = ((), (), s32[]{:S(2)}) async-start(), calls=%async_computation.1 | async-start | bytes 6488064 | tf_op jit(solution)/shard_map/all_gather | solution.py:189
  8.0 310.3 %all-gather.8.cloned.1.call-start = ((), (), s32[]{:S(2)}) async-start(), calls=%async_computation.2 | async-start | bytes 6488064 | tf_op jit(solution)/shard_map/all_gather | solution.py:190
  12.3 134.3 %copy-start.4 = (bf16[4,4,2048]{2,1,0:T(4,128)(2,1)S(1)}, bf16[4,4,2048]{2,1,0:T(4,128)(2,1)}, u32[]{:S(2)}) copy-start(bf16[4,4,2048]{2,1,0:T(4,128)(2,1)} %param.16) | copy-start | bytes 196612
  12.7 138.5 %copy-start.1 = (bf16[2048,64]{0,1:T(8,128)(2,1)S(1)}, bf16[2048,64]{0,1:T(8,128)(2,1)}, u32[]{:S(2)}) copy-start(bf16[2048,64]{0,1:T(8,128)(2,1)} %param.27) | copy-start | bytes 786436
  12.7 138.5 %copy-start.6 = (f32[2048]{0:T(1024)S(1)}, f32[2048]{0:T(1024)}, u32[]{:S(2)}) copy-start(f32[2048]{0:T(1024)} %param.26) | copy-start | bytes 24580
  14.3 12.8 %collective-permute-start = (f32[2,2,2,4,4,514]{5,4,3,2,1,0:T(4,128)S(1)}, f32[2,2,2,4,4,514]{5,4,3,2,1,0:T(4,128)S(1)}, u32[]{:S(2)}, u32[]{:S(2)}) collective-permute-start(f32[2,2,2,4,4,514]{5,4,3,2,1,0:T(4,128)S(1)} %pad_maximum_fusion), channel_id=1, source_target_pairs={{0,256},{8,264},{16,272},{24,280},{32,288},{40,296},{48,304},{56,3... | collective-permute-start | bytes 789512 | tf_op jit(solution)/shard_map/ppermute | solution.py:20
  28.3 10.6 %collective-permute-start.1 = (f32[2,2,4,4,514]{4,3,2,1,0:T(4,128)S(1)}, f32[2,2,4,4,514]{4,3,2,1,0:T(4,128)S(1)}, u32[]{:S(2)}, u32[]{:S(2)}) collective-permute-start(f32[2,2,4,4,514]{4,3,2,1,0:T(4,128)S(1)} %pad_maximum_fusion.1), channel_id=1, source_target_pairs={{0,32},{8,40},{16,48},{24,56},{32,0},{40,8},{48,16},{56,24},{64,96... | collective-permute-start | bytes 394760 | tf_op jit(solution)/shard_map/ppermute | solution.py:20
  39.8 14.9 %collective-permute-start.2 = (f32[2,4,4,514]{3,2,1,0:T(4,128)S(1)}, f32[2,4,4,514]{3,2,1,0:T(4,128)S(1)}, u32[]{:S(2)}, u32[]{:S(2)}) collective-permute-start(f32[2,4,4,514]{3,2,1,0:T(4,128)S(1)} %pad_maximum_fusion.2), channel_id=1, source_target_pairs={{0,64},{8,72},{16,80},{24,88},{32,96},{40,104},{48,112},{56,120},{... | collective-permute-start | bytes 197384 | tf_op jit(solution)/shard_map/ppermute | solution.py:20
  55.5 15.7 %collective-permute-start.3 = (f32[4,4,514]{2,1,0:T(4,128)S(1)}, f32[4,4,514]{2,1,0:T(4,128)S(1)}, u32[]{:S(2)}, u32[]{:S(2)}) collective-permute-start(f32[4,4,514]{2,1,0:T(4,128)S(1)} %pad_maximum_fusion.3), channel_id=1, source_target_pairs={{0,128},{8,136},{16,144},{24,152},{32,160},{40,168},{48,176},{56,1... | collective-permute-start | bytes 98696 | tf_op jit(solution)/shard_map/ppermute | solution.py:20
  71.5 5.9 %collective-permute-start.4 = (f32[4,4,514]{2,1,0:T(4,128)S(1)}, f32[4,4,514]{2,1,0:T(4,128)S(1)}, u32[]{:S(2)}, u32[]{:S(2)}) collective-permute-start(f32[4,4,514]{2,1,0:T(4,128)S(1)} %pad_maximum_fusion.4), channel_id=1, source_target_pairs={{0,16},{8,24},{16,0},{24,8},{32,48},{40,56},{48,32},{56,40},{64,80... | collective-permute-start | bytes 98696 | tf_op jit(solution)/shard_map/ppermute | solution.py:20
  77.7 3.1 collective-permute-start.5
  81.5 3.2 collective-permute-start.6
  84.8 7.5 %collective-permute-start.7 = (f32[16,2048]{1,0:T(8,128)S(1)}, f32[16,2048]{1,0:T(8,128)S(1)}, u32[]{:S(2)}, u32[]{:S(2)}) collective-permute-start(f32[16,2048]{1,0:T(8,128)S(1)} %add.216), channel_id=1, source_target_pairs={{0,16},{8,24},{16,0},{24,8},{32,48},{40,56},{48,32},{56,40},{64,80... | collective-permute-start | bytes 393224 | tf_op jit(solution)/shard_map/ppermute | solution.py:20
  92.3 10.4 %collective-permute-start.8 = (f32[16,2048]{1,0:T(8,128)S(1)}, f32[16,2048]{1,0:T(8,128)S(1)}, u32[]{:S(2)}, u32[]{:S(2)}) collective-permute-start(f32[16,2048]{1,0:T(8,128)S(1)} %add.217), channel_id=1, source_target_pairs={{0,32},{8,40},{16,48},{24,56},{32,0},{40,8},{48,16},{56,24},{64,96... | collective-permute-start | bytes 393224 | tf_op jit(solution)/shard_map/ppermute | solution.py:20
  102.7 18.6 %collective-permute-start.9 = (f32[16,2048]{1,0:T(8,128)S(1)}, f32[16,2048]{1,0:T(8,128)S(1)}, u32[]{:S(2)}, u32[]{:S(2)}) collective-permute-start(f32[16,2048]{1,0:T(8,128)S(1)} %add.218), channel_id=1, source_target_pairs={{0,64},{8,72},{16,80},{24,88},{32,96},{40,104},{48,112},{56,120},{... | collective-permute-start | bytes 393224 | tf_op jit(solution)/shard_map/ppermute | solution.py:20
  121.3 22.9 %collective-permute-start.10 = (f32[16,2048]{1,0:T(8,128)S(1)}, f32[16,2048]{1,0:T(8,128)S(1)}, u32[]{:S(2)}, u32[]{:S(2)}) collective-permute-start(f32[16,2048]{1,0:T(8,128)S(1)} %add.219), channel_id=1, source_target_pairs={{0,128},{8,136},{16,144},{24,152},{32,160},{40,168},{48,176},{56,1... | collective-permute-start | bytes 393224 | tf_op jit(solution)/shard_map/ppermute | solution.py:20
  144.2 6.9 %collective-permute-start.11 = (f32[16,2048]{1,0:T(8,128)S(1)}, f32[16,2048]{1,0:T(8,128)S(1)}, u32[]{:S(2)}, u32[]{:S(2)}) collective-permute-start(f32[16,2048]{1,0:T(8,128)S(1)} %add.220), channel_id=1, source_target_pairs={{0,256},{8,264},{16,272},{24,280},{32,288},{40,296},{48,304},{56,3... | collective-permute-start | bytes 393224 | tf_op jit(solution)/shard_map/ppermute | solution.py:20
  325.7 3.2 collective-permute-start.12
  329.0 7.4 %collective-permute-start.13 = (f32[16,2048]{1,0:T(8,128)S(1)}, f32[16,2048]{1,0:T(8,128)S(1)}, u32[]{:S(2)}, u32[]{:S(2)}) collective-permute-start(f32[16,2048]{1,0:T(8,128)S(1)} %add.226), channel_id=1, source_target_pairs={{0,16},{8,24},{16,0},{24,8},{32,48},{40,56},{48,32},{56,40},{64,80... | collective-permute-start | bytes 393224 | tf_op jit(solution)/shard_map/ppermute | solution.py:20
  336.5 10.3 %collective-permute-start.14 = (f32[16,2048]{1,0:T(8,128)S(1)}, f32[16,2048]{1,0:T(8,128)S(1)}, u32[]{:S(2)}, u32[]{:S(2)}) collective-permute-start(f32[16,2048]{1,0:T(8,128)S(1)} %add.227), channel_id=1, source_target_pairs={{0,32},{8,40},{16,48},{24,56},{32,0},{40,8},{48,16},{56,24},{64,96... | collective-permute-start | bytes 393224 | tf_op jit(solution)/shard_map/ppermute | solution.py:20
  346.8 17.6 %collective-permute-start.15 = (f32[16,2048]{1,0:T(8,128)S(1)}, f32[16,2048]{1,0:T(8,128)S(1)}, u32[]{:S(2)}, u32[]{:S(2)}) collective-permute-start(f32[16,2048]{1,0:T(8,128)S(1)} %add.228), channel_id=1, source_target_pairs={{0,64},{8,72},{16,80},{24,88},{32,96},{40,104},{48,112},{56,120},{... | collective-permute-start | bytes 393224 | tf_op jit(solution)/shard_map/ppermute | solution.py:20
  364.4 24.0 %collective-permute-start.16 = (f32[16,2048]{1,0:T(8,128)S(1)}, f32[16,2048]{1,0:T(8,128)S(1)}, u32[]{:S(2)}, u32[]{:S(2)}) collective-permute-start(f32[16,2048]{1,0:T(8,128)S(1)} %add.229), channel_id=1, source_target_pairs={{0,128},{8,136},{16,144},{24,152},{32,160},{40,168},{48,176},{56,1... | collective-permute-start | bytes 393224 | tf_op jit(solution)/shard_map/ppermute | solution.py:20
  388.4 6.9 %collective-permute-start.17 = (f32[16,2048]{1,0:T(8,128)S(1)}, f32[16,2048]{1,0:T(8,128)S(1)}, u32[]{:S(2)}, u32[]{:S(2)}) collective-permute-start(f32[16,2048]{1,0:T(8,128)S(1)} %add.230), channel_id=1, source_target_pairs={{0,256},{8,264},{16,272},{24,280},{32,288},{40,296},{48,304},{56,3... | collective-permute-start | bytes 393224 | tf_op jit(solution)/shard_map/ppermute | solution.py:20
  (6 other events, 356.2 us)
Sparse Core Ops, SparseCore 0:
  10.5 103.3 all-gather.3
  117.1 100.2 all-gather.5
  220.6 97.7 all-gather.7
where the time goes:
time: 403 us; the launch traced here: 402 us
  waiting for transfers between devices  266 us (66%)
  starting transfers between devices  96.2 us (24%)
  matrix products  15.7 us (4%)
  between operations  13.7 us (3%)
  local copies, waits for them, and re-layouts  6.86 us (2%)
    ppermute x18, waiting for transfers between devices, exchange(): lax.ppermute(part, axis, xor_pairs(count, mask))  102 us
    all_gather x1, waiting for transfers between devices, local(): down_w = lax.all_gather(w_down, 'exp', axis=1, tiled=True)  101 us
    ppermute x18, starting transfers between devices, exchange(): lax.ppermute(part, axis, xor_pairs(count, mask))  96.1 us
    all_gather x1, waiting for transfers between devices, local(): up_w = lax.all_gather(w_up, 'exp', axis=2, tiled=True)  61.2 us
  transfers between devices with their start and end apart: 21, of which 20 were waited for; matrix products, arithmetic and copies ran while one was open for 4% of the time, Pallas kernels for 0%

commit v1 on v0

--- a/solution.py
+++ b/solution.py
@@ -187,7 +187,9 @@
     ).astype(jnp.bfloat16)
     gate_w = lax.all_gather(w_gate, "exp", axis=2, tiled=True)
     up_w = lax.all_gather(w_up, "exp", axis=2, tiled=True)
-    down_w = lax.all_gather(w_down, "exp", axis=1, tiled=True)
+    down_w = jnp.concatenate(
+        lax.all_to_all(jnp.stack([w_down] * lax.axis_size("exp"), axis=0), "exp", 0, 0), axis=1
+    )
     gate = jnp.einsum("erd,edf->erf", dispatched, gate_w, preferred_element_type=jnp.float32)
     upper = jnp.einsum("erd,edf->erf", dispatched, up_w, preferred_element_type=jnp.float32)
     hidden_all = (jax.nn.silu(gate) * upper).astype(jnp.bfloat16)

time: 403 us -> 362 us (0.90)
  waiting for transfers between devices: 266 us -> 217 us
  starting transfers between devices: 96.2 us -> 101 us
    all_gather x1 -> x0, waiting for transfers between devices: 101 us -> none  [local(): down_w = lax.all_gather(w_down, 'exp', axis=1, tiled=True)]
    all_gather x1, waiting for transfers between devices: 61.2 us -> 96.7 us  [local(): up_w = lax.all_gather(w_up, 'exp', axis=2, tiled=True)]
    all_gather x1, waiting for transfers between devices: 0.02 us -> 19.7 us  [local(): gate_w = lax.all_gather(w_gate, 'exp', axis=2, tiled=True)]
    all_to_all x0 -> x1, starting transfers between devices: none -> 4.85 us  [local(): lax.all_to_all(jnp.stack([w_down] * lax.axis_size('exp'), axis=0), 'exp',...]
  transfers between devices with their start and end apart: 21 -> 21, of which waited for: 20 -> 19; matrix products, arithmetic and copies ran while one was open for 4% -> 6% of each run, Pallas kernels for 0% -> 0%
where the time goes in v1:
time: 362 us; the launch traced here: 361 us
  waiting for transfers between devices  217 us (60%)
  starting transfers between devices  101 us (28%)
  matrix products  15.7 us (4%)
  between operations  14 us (4%)
  local copies, waits for them, and re-layouts  10.1 us (3%)
    ppermute x18, waiting for transfers between devices, exchange(): lax.ppermute(part, axis, xor_pairs(count, mask))  99.5 us
    all_gather x1, waiting for transfers between devices, local(): up_w = lax.all_gather(w_up, 'exp', axis=2, tiled=True)  96.7 us
    ppermute x18, starting transfers between devices, exchange(): lax.ppermute(part, axis, xor_pairs(count, mask))  95.7 us
    all_gather x1, waiting for transfers between devices, local(): gate_w = lax.all_gather(w_gate, 'exp', axis=2, tiled=True)  19.7 us
  transfers between devices with their start and end apart: 21, of which 19 were waited for; matrix products, arithmetic and copies ran while one was open for 6% of the time, Pallas kernels for 0%

profile of v1, /device:TPU:8, one launch (start us, length us, event | category | flops | bytes accessed | tf_op | source)
XLA Modules:
  0.0 361.3 jit_solution(1965306934168135428)
XLA Ops:
  13.4 7.7 %collective-permute-start = (f32[2,2,2,4,4,514]{5,4,3,2,1,0:T(4,128)S(1)}, f32[2,2,2,4,4,514]{5,4,3,2,1,0:T(4,128)S(1)}, u32[]{:S(2)}, u32[]{:S(2)}) collective-permute-start(f32[2,2,2,4,4,514]{5,4,3,2,1,0:T(4,128)S(1)} %pad_maximum_fusion), channel_id=1, source_target_pairs={{0,256},{8,264},{16,272},{24,280},{32,288},{40,296},{48,304},{56,3... | collective-permute-start | bytes 789512 | tf_op jit(solution)/shard_map/ppermute | solution.py:20
  24.4 4.8 %all-to-all-start = ((bf16[8,1,176,2048]{3,2,1,0:T(8,128)(2,1)}), bf16[8,1,176,2048]{3,2,1,0:T(8,128)(2,1)}, u32[]{:S(2)}, u32[]{:S(2)}) async-start(bf16[8,1,176,2048]{3,2,1,0:T(8,128)(2,1)} %stack.2), calls=%async_computation | async-start | bytes 11534336 | tf_op jit(solution)/shard_map/all_to_all | solution.py:191
  33.6 6.5 %collective-permute-done.1 = f32[2,2,4,4,514]{4,3,2,1,0:T(4,128)S(1)} collective-permute-done((f32[2,2,4,4,514]{4,3,2,1,0:T(4,128)S(1)}, f32[2,2,4,4,514]{4,3,2,1,0:T(4,128)S(1)}, u32[]{:S(2)}, u32[]{:S(2)}) %collective-permute-start.1) | collective-permute-done | bytes 131616 | tf_op jit(solution)/shard_map/ppermute | solution.py:20
  41.1 9.1 %collective-permute-start.2 = (f32[2,4,4,514]{3,2,1,0:T(4,128)S(1)}, f32[2,4,4,514]{3,2,1,0:T(4,128)S(1)}, u32[]{:S(2)}, u32[]{:S(2)}) collective-permute-start(f32[2,4,4,514]{3,2,1,0:T(4,128)S(1)} %pad_maximum_fusion.2), channel_id=1, source_target_pairs={{0,64},{8,72},{16,80},{24,88},{32,96},{40,104},{48,112},{56,120},{... | collective-permute-start | bytes 197384 | tf_op jit(solution)/shard_map/ppermute | solution.py:20
  51.0 5.0 %collective-permute-done.2 = f32[2,4,4,514]{3,2,1,0:T(4,128)S(1)} collective-permute-done((f32[2,4,4,514]{3,2,1,0:T(4,128)S(1)}, f32[2,4,4,514]{3,2,1,0:T(4,128)S(1)}, u32[]{:S(2)}, u32[]{:S(2)}) %collective-permute-start.2) | collective-permute-done | bytes 65824 | tf_op jit(solution)/shard_map/ppermute | solution.py:20
  56.7 13.7 %collective-permute-start.3 = (f32[4,4,514]{2,1,0:T(4,128)S(1)}, f32[4,4,514]{2,1,0:T(4,128)S(1)}, u32[]{:S(2)}, u32[]{:S(2)}) collective-permute-start(f32[4,4,514]{2,1,0:T(4,128)S(1)} %pad_maximum_fusion.3), channel_id=1, source_target_pairs={{0,128},{8,136},{16,144},{24,152},{32,160},{40,168},{48,176},{56,1... | collective-permute-start | bytes 98696 | tf_op jit(solution)/shard_map/ppermute | solution.py:20
  88.0 5.5 %collective-permute-done.7 = f32[16,2048]{1,0:T(8,128)S(1)} collective-permute-done((f32[16,2048]{1,0:T(8,128)S(1)}, f32[16,2048]{1,0:T(8,128)S(1)}, u32[]{:S(2)}, u32[]{:S(2)}) %collective-permute-start.7) | collective-permute-done | bytes 131104 | tf_op jit(solution)/shard_map/ppermute | solution.py:20
  95.5 8.5 %collective-permute-done.8 = f32[16,2048]{1,0:T(8,128)S(1)} collective-permute-done((f32[16,2048]{1,0:T(8,128)S(1)}, f32[16,2048]{1,0:T(8,128)S(1)}, u32[]{:S(2)}, u32[]{:S(2)}) %collective-permute-start.8) | collective-permute-done | bytes 131104 | tf_op jit(solution)/shard_map/ppermute | solution.py:20
  104.0 6.4 %collective-permute-start.9 = (f32[16,2048]{1,0:T(8,128)S(1)}, f32[16,2048]{1,0:T(8,128)S(1)}, u32[]{:S(2)}, u32[]{:S(2)}) collective-permute-start(f32[16,2048]{1,0:T(8,128)S(1)} %add.218), channel_id=1, source_target_pairs={{0,64},{8,72},{16,80},{24,88},{32,96},{40,104},{48,112},{56,120},{... | collective-permute-start | bytes 393224 | tf_op jit(solution)/shard_map/ppermute | solution.py:20
  110.4 12.2 %collective-permute-done.9 = f32[16,2048]{1,0:T(8,128)S(1)} collective-permute-done((f32[16,2048]{1,0:T(8,128)S(1)}, f32[16,2048]{1,0:T(8,128)S(1)}, u32[]{:S(2)}, u32[]{:S(2)}) %collective-permute-start.9) | collective-permute-done | bytes 131104 | tf_op jit(solution)/shard_map/ppermute | solution.py:20
  122.6 10.5 %collective-permute-start.10 = (f32[16,2048]{1,0:T(8,128)S(1)}, f32[16,2048]{1,0:T(8,128)S(1)}, u32[]{:S(2)}, u32[]{:S(2)}) collective-permute-start(f32[16,2048]{1,0:T(8,128)S(1)} %add.219), channel_id=1, source_target_pairs={{0,128},{8,136},{16,144},{24,152},{32,160},{40,168},{48,176},{56,1... | collective-permute-start | bytes 393224 | tf_op jit(solution)/shard_map/ppermute | solution.py:20
  133.1 12.3 %collective-permute-done.10 = f32[16,2048]{1,0:T(8,128)S(1)} collective-permute-done((f32[16,2048]{1,0:T(8,128)S(1)}, f32[16,2048]{1,0:T(8,128)S(1)}, u32[]{:S(2)}, u32[]{:S(2)}) %collective-permute-start.10) | collective-permute-done | bytes 131104 | tf_op jit(solution)/shard_map/ppermute | solution.py:20
  150.1 5.2 %collective-permute-done.11 = f32[16,2048]{1,0:T(8,128)S(1)} collective-permute-done((f32[16,2048]{1,0:T(8,128)S(1)}, f32[16,2048]{1,0:T(8,128)S(1)}, u32[]{:S(2)}, u32[]{:S(2)}) %collective-permute-start.11) | collective-permute-done | bytes 131104 | tf_op jit(solution)/shard_map/ppermute | solution.py:20
  156.2 19.7 %all-gather.3.cloned.1.call-done = bf16[1,2048,1408]{1,2,0:T(8,128)(2,1)} async-done(((bf16[1,2048,176]{1,2,0:T(8,128)(2,1)}), bf16[1,2048,1408]{1,2,0:T(8,128)(2,1)}) %all-gather.3.cloned.1.call-update) | async-done | bytes 5767184 | tf_op jit(solution)/shard_map/all_gather | solution.py:188
  175.9 4.2 %fusion.2 = f32[3,1408]{1,0:T(4,128)S(1)} fusion(bf16[3,2048]{1,0:T(4,128)(2,1)S(1)} %convolution_convert_fusion, bf16[1,2048,1408]{1,2,0:T(8,128)(2,1)} %all-gather.3.cloned.1.call-done), kind=kOutput, calls=%fused_computation.2 | convolution fusion | flops 17301504 | bytes 5796352 | tf_op jit(solution)/shard_map/erd,edf->erf/dot_general | solution.py:193
  180.1 96.7 %all-gather.5.cloned.1.call-done = bf16[1,2048,1408]{1,2,0:T(8,128)(2,1)} async-done(((bf16[1,2048,176]{1,2,0:T(8,128)(2,1)}), bf16[1,2048,1408]{1,2,0:T(8,128)(2,1)}) %all-gather.5.cloned.1.call-update) | async-done | bytes 5767184 | tf_op jit(solution)/shard_map/all_gather | solution.py:189
  276.9 7.0 %fusion.13 = f32[3,2048]{1,0:T(4,128)S(1)} fusion(bf16[1408,2048]{1,0:T(8,128)(2,1)} %bitcast.51, bf16[3,2048]{1,0:T(4,128)(2,1)S(1)} %convolution_convert_fusion, bf16[1,2048,1408]{1,2,0:T(8,128)(2,1)} %all-gather.5.cloned.1.call-done, f32[3,1408]{1,0:T(4,128)S(1)} %fusion.2), kind=kOutput, calls=%fused_computation.11 | convolution fusion | flops 34628352 | bytes 11588096 | tf_op jit(solution)/shard_map/erf,efd->erd/dot_general | solution.py:196
  291.0 4.0 %collective-permute-done.13 = f32[16,2048]{1,0:T(8,128)S(1)} collective-permute-done((f32[16,2048]{1,0:T(8,128)S(1)}, f32[16,2048]{1,0:T(8,128)S(1)}, u32[]{:S(2)}, u32[]{:S(2)}) %collective-permute-start.13) | collective-permute-done | bytes 131104 | tf_op jit(solution)/shard_map/ppermute | solution.py:20
  295.0 4.5 %collective-permute-start.14 = (f32[16,2048]{1,0:T(8,128)S(1)}, f32[16,2048]{1,0:T(8,128)S(1)}, u32[]{:S(2)}, u32[]{:S(2)}) collective-permute-start(f32[16,2048]{1,0:T(8,128)S(1)} %add.227), channel_id=1, source_target_pairs={{0,32},{8,40},{16,48},{24,56},{32,0},{40,8},{48,16},{56,24},{64,96... | collective-permute-start | bytes 393224 | tf_op jit(solution)/shard_map/ppermute | solution.py:20
  299.4 5.8 %collective-permute-done.14 = f32[16,2048]{1,0:T(8,128)S(1)} collective-permute-done((f32[16,2048]{1,0:T(8,128)S(1)}, f32[16,2048]{1,0:T(8,128)S(1)}, u32[]{:S(2)}, u32[]{:S(2)}) %collective-permute-start.14) | collective-permute-done | bytes 131104 | tf_op jit(solution)/shard_map/ppermute | solution.py:20
  305.3 7.6 %collective-permute-start.15 = (f32[16,2048]{1,0:T(8,128)S(1)}, f32[16,2048]{1,0:T(8,128)S(1)}, u32[]{:S(2)}, u32[]{:S(2)}) collective-permute-start(f32[16,2048]{1,0:T(8,128)S(1)} %add.228), channel_id=1, source_target_pairs={{0,64},{8,72},{16,80},{24,88},{32,96},{40,104},{48,112},{56,120},{... | collective-permute-start | bytes 393224 | tf_op jit(solution)/shard_map/ppermute | solution.py:20
  312.9 9.9 %collective-permute-done.15 = f32[16,2048]{1,0:T(8,128)S(1)} collective-permute-done((f32[16,2048]{1,0:T(8,128)S(1)}, f32[16,2048]{1,0:T(8,128)S(1)}, u32[]{:S(2)}, u32[]{:S(2)}) %collective-permute-start.15) | collective-permute-done | bytes 131104 | tf_op jit(solution)/shard_map/ppermute | solution.py:20
  322.9 12.0 %collective-permute-start.16 = (f32[16,2048]{1,0:T(8,128)S(1)}, f32[16,2048]{1,0:T(8,128)S(1)}, u32[]{:S(2)}, u32[]{:S(2)}) collective-permute-start(f32[16,2048]{1,0:T(8,128)S(1)} %add.229), channel_id=1, source_target_pairs={{0,128},{8,136},{16,144},{24,152},{32,160},{40,168},{48,176},{56,1... | collective-permute-start | bytes 393224 | tf_op jit(solution)/shard_map/ppermute | solution.py:20
  334.9 12.0 %collective-permute-done.16 = f32[16,2048]{1,0:T(8,128)S(1)} collective-permute-done((f32[16,2048]{1,0:T(8,128)S(1)}, f32[16,2048]{1,0:T(8,128)S(1)}, u32[]{:S(2)}, u32[]{:S(2)}) %collective-permute-start.16) | collective-permute-done | bytes 131104 | tf_op jit(solution)/shard_map/ppermute | solution.py:20
  (144 shorter events, 56.2 us)
Async XLA Ops:
  6.5 169.4 %all-gather.3.cloned.1.call-start = ((), (), s32[]{:S(2)}) async-start(), calls=%async_computation.1 | async-start | bytes 6488064 | tf_op jit(solution)/shard_map/all_gather | solution.py:188
  7.3 269.6 %all-gather.5.cloned.1.call-start = ((), (), s32[]{:S(2)}) async-start(), calls=%async_computation.2 | async-start | bytes 6488064 | tf_op jit(solution)/shard_map/all_gather | solution.py:189
  13.4 16.9 %collective-permute-start = (f32[2,2,2,4,4,514]{5,4,3,2,1,0:T(4,128)S(1)}, f32[2,2,2,4,4,514]{5,4,3,2,1,0:T(4,128)S(1)}, u32[]{:S(2)}, u32[]{:S(2)}) collective-permute-start(f32[2,2,2,4,4,514]{5,4,3,2,1,0:T(4,128)S(1)} %pad_maximum_fusion), channel_id=1, source_target_pairs={{0,256},{8,264},{16,272},{24,280},{32,288},{40,296},{48,304},{56,3... | collective-permute-start | bytes 789512 | tf_op jit(solution)/shard_map/ppermute | solution.py:20
  24.4 155.8 %all-to-all-start = ((bf16[8,1,176,2048]{3,2,1,0:T(8,128)(2,1)}), bf16[8,1,176,2048]{3,2,1,0:T(8,128)(2,1)}, u32[]{:S(2)}, u32[]{:S(2)}) async-start(bf16[8,1,176,2048]{3,2,1,0:T(8,128)(2,1)} %stack.2), calls=%async_computation | async-start | bytes 11534336 | tf_op jit(solution)/shard_map/all_to_all | solution.py:191
  29.3 120.2 %copy-start.5 = (bf16[4,4,2048]{2,1,0:T(4,128)(2,1)S(1)}, bf16[4,4,2048]{2,1,0:T(4,128)(2,1)}, u32[]{:S(2)}) copy-start(bf16[4,4,2048]{2,1,0:T(4,128)(2,1)} %param.16) | copy-start | bytes 196612
  29.3 126.2 %copy-start.2 = (bf16[2048,64]{0,1:T(8,128)(2,1)S(1)}, bf16[2048,64]{0,1:T(8,128)(2,1)}, u32[]{:S(2)}) copy-start(bf16[2048,64]{0,1:T(8,128)(2,1)} %param.27) | copy-start | bytes 786436
  29.3 126.2 %copy-start.7 = (f32[2048]{0:T(1024)S(1)}, f32[2048]{0:T(1024)}, u32[]{:S(2)}) copy-start(f32[2048]{0:T(1024)} %param.26) | copy-start | bytes 24580
  31.6 8.6 %collective-permute-start.1 = (f32[2,2,4,4,514]{4,3,2,1,0:T(4,128)S(1)}, f32[2,2,4,4,514]{4,3,2,1,0:T(4,128)S(1)}, u32[]{:S(2)}, u32[]{:S(2)}) collective-permute-start(f32[2,2,4,4,514]{4,3,2,1,0:T(4,128)S(1)} %pad_maximum_fusion.1), channel_id=1, source_target_pairs={{0,32},{8,40},{16,48},{24,56},{32,0},{40,8},{48,16},{56,24},{64,96... | collective-permute-start | bytes 394760 | tf_op jit(solution)/shard_map/ppermute | solution.py:20
  41.1 14.9 %collective-permute-start.2 = (f32[2,4,4,514]{3,2,1,0:T(4,128)S(1)}, f32[2,4,4,514]{3,2,1,0:T(4,128)S(1)}, u32[]{:S(2)}, u32[]{:S(2)}) collective-permute-start(f32[2,4,4,514]{3,2,1,0:T(4,128)S(1)} %pad_maximum_fusion.2), channel_id=1, source_target_pairs={{0,64},{8,72},{16,80},{24,88},{32,96},{40,104},{48,112},{56,120},{... | collective-permute-start | bytes 197384 | tf_op jit(solution)/shard_map/ppermute | solution.py:20
  56.7 15.7 %collective-permute-start.3 = (f32[4,4,514]{2,1,0:T(4,128)S(1)}, f32[4,4,514]{2,1,0:T(4,128)S(1)}, u32[]{:S(2)}, u32[]{:S(2)}) collective-permute-start(f32[4,4,514]{2,1,0:T(4,128)S(1)} %pad_maximum_fusion.3), channel_id=1, source_target_pairs={{0,128},{8,136},{16,144},{24,152},{32,160},{40,168},{48,176},{56,1... | collective-permute-start | bytes 98696 | tf_op jit(solution)/shard_map/ppermute | solution.py:20
  72.8 5.9 %collective-permute-start.4 = (f32[4,4,514]{2,1,0:T(4,128)S(1)}, f32[4,4,514]{2,1,0:T(4,128)S(1)}, u32[]{:S(2)}, u32[]{:S(2)}) collective-permute-start(f32[4,4,514]{2,1,0:T(4,128)S(1)} %pad_maximum_fusion.4), channel_id=1, source_target_pairs={{0,16},{8,24},{16,0},{24,8},{32,48},{40,56},{48,32},{56,40},{64,80... | collective-permute-start | bytes 98696 | tf_op jit(solution)/shard_map/ppermute | solution.py:20
  79.0 3.1 collective-permute-start.5
  82.8 3.2 collective-permute-start.6
  86.0 7.5 %collective-permute-start.7 = (f32[16,2048]{1,0:T(8,128)S(1)}, f32[16,2048]{1,0:T(8,128)S(1)}, u32[]{:S(2)}, u32[]{:S(2)}) collective-permute-start(f32[16,2048]{1,0:T(8,128)S(1)} %add.216), channel_id=1, source_target_pairs={{0,16},{8,24},{16,0},{24,8},{32,48},{40,56},{48,32},{56,40},{64,80... | collective-permute-start | bytes 393224 | tf_op jit(solution)/shard_map/ppermute | solution.py:20
  93.5 10.4 %collective-permute-start.8 = (f32[16,2048]{1,0:T(8,128)S(1)}, f32[16,2048]{1,0:T(8,128)S(1)}, u32[]{:S(2)}, u32[]{:S(2)}) collective-permute-start(f32[16,2048]{1,0:T(8,128)S(1)} %add.217), channel_id=1, source_target_pairs={{0,32},{8,40},{16,48},{24,56},{32,0},{40,8},{48,16},{56,24},{64,96... | collective-permute-start | bytes 393224 | tf_op jit(solution)/shard_map/ppermute | solution.py:20
  104.0 18.6 %collective-permute-start.9 = (f32[16,2048]{1,0:T(8,128)S(1)}, f32[16,2048]{1,0:T(8,128)S(1)}, u32[]{:S(2)}, u32[]{:S(2)}) collective-permute-start(f32[16,2048]{1,0:T(8,128)S(1)} %add.218), channel_id=1, source_target_pairs={{0,64},{8,72},{16,80},{24,88},{32,96},{40,104},{48,112},{56,120},{... | collective-permute-start | bytes 393224 | tf_op jit(solution)/shard_map/ppermute | solution.py:20
  122.6 22.9 %collective-permute-start.10 = (f32[16,2048]{1,0:T(8,128)S(1)}, f32[16,2048]{1,0:T(8,128)S(1)}, u32[]{:S(2)}, u32[]{:S(2)}) collective-permute-start(f32[16,2048]{1,0:T(8,128)S(1)} %add.219), channel_id=1, source_target_pairs={{0,128},{8,136},{16,144},{24,152},{32,160},{40,168},{48,176},{56,1... | collective-permute-start | bytes 393224 | tf_op jit(solution)/shard_map/ppermute | solution.py:20
  145.5 9.8 %collective-permute-start.11 = (f32[16,2048]{1,0:T(8,128)S(1)}, f32[16,2048]{1,0:T(8,128)S(1)}, u32[]{:S(2)}, u32[]{:S(2)}) collective-permute-start(f32[16,2048]{1,0:T(8,128)S(1)} %add.220), channel_id=1, source_target_pairs={{0,256},{8,264},{16,272},{24,280},{32,288},{40,296},{48,304},{56,3... | collective-permute-start | bytes 393224 | tf_op jit(solution)/shard_map/ppermute | solution.py:20
  284.3 3.2 collective-permute-start.12
  287.5 7.4 %collective-permute-start.13 = (f32[16,2048]{1,0:T(8,128)S(1)}, f32[16,2048]{1,0:T(8,128)S(1)}, u32[]{:S(2)}, u32[]{:S(2)}) collective-permute-start(f32[16,2048]{1,0:T(8,128)S(1)} %add.226), channel_id=1, source_target_pairs={{0,16},{8,24},{16,0},{24,8},{32,48},{40,56},{48,32},{56,40},{64,80... | collective-permute-start | bytes 393224 | tf_op jit(solution)/shard_map/ppermute | solution.py:20
  295.0 10.3 %collective-permute-start.14 = (f32[16,2048]{1,0:T(8,128)S(1)}, f32[16,2048]{1,0:T(8,128)S(1)}, u32[]{:S(2)}, u32[]{:S(2)}) collective-permute-start(f32[16,2048]{1,0:T(8,128)S(1)} %add.227), channel_id=1, source_target_pairs={{0,32},{8,40},{16,48},{24,56},{32,0},{40,8},{48,16},{56,24},{64,96... | collective-permute-start | bytes 393224 | tf_op jit(solution)/shard_map/ppermute | solution.py:20
  305.3 17.6 %collective-permute-start.15 = (f32[16,2048]{1,0:T(8,128)S(1)}, f32[16,2048]{1,0:T(8,128)S(1)}, u32[]{:S(2)}, u32[]{:S(2)}) collective-permute-start(f32[16,2048]{1,0:T(8,128)S(1)} %add.228), channel_id=1, source_target_pairs={{0,64},{8,72},{16,80},{24,88},{32,96},{40,104},{48,112},{56,120},{... | collective-permute-start | bytes 393224 | tf_op jit(solution)/shard_map/ppermute | solution.py:20
  322.9 24.0 %collective-permute-start.16 = (f32[16,2048]{1,0:T(8,128)S(1)}, f32[16,2048]{1,0:T(8,128)S(1)}, u32[]{:S(2)}, u32[]{:S(2)}) collective-permute-start(f32[16,2048]{1,0:T(8,128)S(1)} %add.229), channel_id=1, source_target_pairs={{0,128},{8,136},{16,144},{24,152},{32,160},{40,168},{48,176},{56,1... | collective-permute-start | bytes 393224 | tf_op jit(solution)/shard_map/ppermute | solution.py:20
  346.9 6.9 %collective-permute-start.17 = (f32[16,2048]{1,0:T(8,128)S(1)}, f32[16,2048]{1,0:T(8,128)S(1)}, u32[]{:S(2)}, u32[]{:S(2)}) collective-permute-start(f32[16,2048]{1,0:T(8,128)S(1)} %add.230), channel_id=1, source_target_pairs={{0,256},{8,264},{16,272},{24,280},{32,288},{40,296},{48,304},{56,3... | collective-permute-start | bytes 393224 | tf_op jit(solution)/shard_map/ppermute | solution.py:20
  (7 other events, 296.4 us)
Sparse Core Ops, SparseCore 0:
  10.5 165.3 all-gather.2
  179.1 97.7 all-gather.4
